TPU v7x, 32 devices: a whole 2x2x4 slice. The times are simulated.
32 devices in a mesh: fsdp: 4 (over y, x), seq: 8 (over z, core).
Axes of the slice: x: 2, y: 2, z: 4, core: 2. Of those that a mesh axis runs over, the one named last changes fastest.
Arguments:
- events: bfloat16 [4, 1024, 2048], P('fsdp', 'seq'), may hold values from -6 to 6
- type_ids: int32 [4, 1024], P('fsdp', 'seq'), may hold values from 0 to 255
- type_table: bfloat16 [256, 2048], P('fsdp'), may hold values from -6 to 6
- norm_gain: float32 [2048], replicated, may hold values from 0.25 to 1.75
- kernel: bfloat16 [2048, 1152], P('fsdp'), may hold values from -0.1875 to 0.1875
- upstream: bfloat16 [4, 1024, 2048], P('fsdp', 'seq'), may hold values from -6 to 6
Outputs:
- input_grad: bfloat16 [4, 1024, 2048], P('fsdp', 'seq')
- table_grad: float32 [256, 2048], P(('fsdp', 'seq'))
- gain_grad: float32 [2048], P(('fsdp', 'seq'))
- kernel_grad: float32 [2048, 1152], P('seq')
All inputs are finite; a program needn't handle non-finite values.
Results may differ from a plain program's by a relative error of at most 0.0053.
Values may be sent and summed in bfloat16 or wider, within the bound.
No kernel may reach another device: no remote copies, remote signals or barrier semaphores. Data moves between devices by JAX's collectives and lax.ppermute only.
A program may use at most 128 MiB of HBM per device.

v0:
```python
import jax
import jax.numpy as jnp
from jax import lax
from jax.sharding import PartitionSpec as P

GROUPS = 16
KERNEL = 9


def with_halo(cells, sides, width):
    for axis, dim in sides:
        count = lax.axis_size(axis)
        ends = count - 1
        head = lax.slice_in_dim(cells, 0, width, axis=dim)
        tail = lax.slice_in_dim(cells, cells.shape[dim] - width, cells.shape[dim], axis=dim)
        cells = jnp.concatenate(
            [
                lax.ppermute(tail, axis, [(i, (i + 1) % count) for i in range(ends)]),
                cells,
                lax.ppermute(head, axis, [((i + 1) % count, i) for i in range(ends)]),
            ],
            axis=dim,
        )
    return cells


def from_partner(value, axis, apart):
    mask = 2**apart
    pairs = [(source, source ^ mask) for source in range(lax.axis_size(axis))]
    return lax.ppermute(value, axis, pairs)


def body(events, type_ids, type_table, norm_gain, kernel, upstream):
    length = events.shape[1]
    width = events.shape[2]
    chans = width // GROUPS
    half = KERNEL // 2
    seq_count = lax.axis_size("seq")
    total = length * seq_count * lax.axis_size("fsdp")
    scale = 1.0 / jnp.sqrt(jnp.float32(total))
    table = lax.all_gather(type_table, "fsdp", axis=0, tiled=True)
    onehot = (type_ids[0][:, None] == jnp.arange(table.shape[0], dtype=jnp.int32)[None, :]).astype(
        jnp.bfloat16
    )
    mixed = events[0].astype(jnp.float32) + jnp.dot(
        onehot, table, preferred_element_type=jnp.float32
    )
    inv = lax.rsqrt(jnp.mean(mixed * mixed, axis=-1, keepdims=True) + 1e-06)
    normed = (mixed * inv * norm_gain).astype(jnp.bfloat16)
    padded = with_halo(normed, (("seq", 0),), half)
    padded = padded.reshape(length + 2 * half, GROUPS, chans)
    weights = lax.all_gather(kernel, "fsdp", axis=0, tiled=True).reshape(
        GROUPS, chans, KERNEL, chans
    )
    conv = jnp.zeros((length, GROUPS, chans), jnp.float32)
    for k in range(KERNEL):
        conv = conv + jnp.einsum(
            "tgc,goc->tgo",
            padded[k : k + length],
            weights[:, :, k, :],
            preferred_element_type=jnp.float32,
        )
    up_float = upstream[0].astype(jnp.float32)
    sig = jax.nn.sigmoid(conv)
    dconv = (up_float.reshape(length, GROUPS, chans) * sig * (1.0 + conv * (1.0 - sig))).astype(
        jnp.bfloat16
    )
    dflat = dconv.reshape(length, width)
    dpad = with_halo(dflat, (("seq", 0),), half)
    dpad = dpad.reshape(length + 2 * half, GROUPS, chans)
    dnormed = jnp.zeros((length, GROUPS, chans), jnp.float32)
    for k in range(KERNEL):
        dnormed = dnormed + jnp.einsum(
            "tgo,goc->tgc",
            dpad[2 * half - k : 2 * half - k + length],
            weights[:, :, k, :],
            preferred_element_type=jnp.float32,
        )
    slice_width = width // seq_count
    normed_slice, dconv_slice = (
        lax.all_to_all(normed, "seq", split_axis=1, concat_axis=0, tiled=True),
        lax.all_to_all(dflat, "seq", split_axis=1, concat_axis=0, tiled=True),
    )
    whole = normed_slice.shape[0]
    if slice_width < chans:
        spread = chans // slice_width
        position = lax.axis_index("seq")
        group_rows = normed_slice
        for bit in range(spread.bit_length() - 1):
            partner = from_partner(group_rows, "seq", bit)
            lower = position >> bit & 1 == 0
            group_rows = jnp.where(
                lower,
                jnp.concatenate([group_rows, partner], axis=1),
                jnp.concatenate([partner, group_rows], axis=1),
            )
        group_in = group_rows.reshape(whole, 1, chans)
        group_out = dconv_slice.reshape(whole, 1, slice_width)
    else:
        local_groups = slice_width // chans
        group_in = normed_slice.reshape(whole, local_groups, chans)
        group_out = dconv_slice.reshape(whole, local_groups, chans)
    group_pad = jnp.pad(group_in, ((half, half), (0, 0), (0, 0)))
    kterms = []
    for k in range(KERNEL):
        kterms.append(
            jnp.einsum(
                "tgo,tgc->goc",
                group_out,
                group_pad[k : k + whole],
                preferred_element_type=jnp.float32,
            )
        )
    kernel_part = jnp.stack(kterms, axis=2).reshape(slice_width, KERNEL * chans) * scale
    kernel_grad = lax.psum(kernel_part, "fsdp")
    dnormed = dnormed.reshape(length, width)
    gain_term = jnp.sum(dnormed * mixed * inv, axis=0) * scale
    scaled = norm_gain * dnormed
    dmixed = inv * scaled - mixed * inv * inv * inv * jnp.mean(
        scaled * mixed, axis=-1, keepdims=True
    )
    input_grad = (up_float + dmixed).astype(jnp.bfloat16)
    table_term = (
        lax.dot_general(
            onehot, input_grad, (((0,), (0,)), ((), ())), preferred_element_type=jnp.float32
        )
        * scale
    )
    table_grad, gain_grad = (
        lax.psum_scatter(table_term, ("fsdp", "seq"), scatter_dimension=0, tiled=True),
        lax.psum_scatter(gain_term, ("fsdp", "seq"), scatter_dimension=0, tiled=True),
    )
    return (input_grad[None], table_grad, gain_grad, kernel_grad)


def solution(mesh):
    return jax.shard_map(
        body,
        mesh=mesh,
        in_specs=(
            P("fsdp", "seq", None),
            P("fsdp", "seq"),
            P("fsdp", None),
            P(),
            P("fsdp", None),
            P("fsdp", "seq", None),
        ),
        out_specs=(
            P("fsdp", "seq", None),
            P(("fsdp", "seq"), None),
            P(("fsdp", "seq")),
            P("seq", None),
        ),
        check_vma=False,
    )
```

profile of v0, /device:TPU:0, one launch (start us, length us, event | category | flops | bytes accessed | tf_op | source)
XLA Modules:
  0.0 384.2 jit_solution(598750002941307094)
XLA Ops:
  7.2 0.7 all-gather.3.cloned.1.call-update
  8.0 0.7 all-gather.5.cloned.1.call-update
  8.7 30.6 %all-gather.3.cloned.1.call-done = bf16[256,2048]{1,0:T(8,128)(2,1)} async-done(((bf16[64,2048]{1,0:T(8,128)(2,1)}), bf16[256,2048]{1,0:T(8,128)(2,1)}) %all-gather.3.cloned.1.call-update) | async-done | bytes 1048592 | tf_op jit(solution)/shard_map/all_gather | solution.py:41
  39.2 1.7 multiply_reduce_fusion.2
  41.1 1.0 copy.192
  42.1 4.6 %all-to-all-start.1 = ((bf16[128,8,256]{0,2,1:T(8,128)(2,1)}), bf16[128,8,256]{0,2,1:T(8,128)(2,1)S(1)}, u32[]{:S(2)}, u32[]{:S(2)}) async-start(bf16[128,8,256]{0,2,1:T(8,128)(2,1)} %bitcast.30), calls=%async_computation.2 | async-start | bytes 1048576 | tf_op jit(solution)/shard_map/all_to_all | solution.py:81
  46.7 2.4 collective-permute-start
  49.1 1.3 collective-permute-start.1
  50.6 1.2 copy.213
  51.7 1.6 collective-permute-done.1
  53.4 2.7 fusion.52
  56.0 6.0 %all-to-all-done.1 = bf16[128,8,256]{0,2,1:T(8,128)(2,1)S(1)} async-done(((bf16[128,8,256]{0,2,1:T(8,128)(2,1)}), bf16[128,8,256]{0,2,1:T(8,128)(2,1)S(1)}, u32[]{:S(2)}, u32[]{:S(2)}) %all-to-all-start.1) | async-done | bytes 524320 | tf_op jit(solution)/shard_map/all_to_all | solution.py:81
  62.6 1.0 copy.169
  63.7 34.5 %all-gather.5.cloned.1.call-done = bf16[2048,1152]{1,0:T(8,128)(2,1)} async-done(((bf16[512,1152]{1,0:T(8,128)(2,1)}), bf16[2048,1152]{1,0:T(8,128)(2,1)}) %all-gather.5.cloned.1.call-update) | async-done | bytes 4718608 | tf_op jit(solution)/shard_map/all_gather | solution.py:52
  98.2 10.5 %reshape.88 = bf16[16,128,9,128]{3,2,1,0:T(8,128)(2,1)} reshape(bf16[2048,1152]{1,0:T(8,128)(2,1)} %all-gather.5.cloned.1.call-done) | data formatting | bytes 9437184 | tf_op jit(solution)/shard_map/reshape | solution.py:52
  108.6 19.8 %fusion.82 = (bf16[16,128,1,128]{3,2,1,0:T(2,128)(2,1)S(1)}, bf16[16,128,1,128]{3,2,1,0:T(2,128)(2,1)S(1)}, bf16[16,128,1,128]{3,2,1,0:T(2,128)(2,1)S(1)}, bf16[...) fusion(bf16[16,128,9,128]{3,2,1,0:T(8,128)(2,1)} %reshape.88), kind=kLoop, calls=%fused_computation.154 | loop fusion | bytes 9437184 | tf_op jit(solution)/shard_map/slice | solution.py:60
  129.0 0.9 copy-done.22
  130.5 0.9 copy-done.21
  131.8 0.7 copy-done.20
  136.1 0.7 copy-done.25
  137.0 0.8 fusion.14
  137.9 1.1 copy.145
  138.9 1.3 collective-permute-start.2
  140.2 1.1 copy.155
  141.3 3.8 collective-permute-start.3
  145.1 2.7 fusion.63
  147.8 1.0 copy.144
  148.8 4.7 %all-to-all-start = ((bf16[128,8,256]{0,2,1:T(8,128)(2,1)}), bf16[128,8,256]{0,2,1:T(8,128)(2,1)S(1)}, u32[]{:S(2)}, u32[]{:S(2)}) async-start(bf16[128,8,256]{0,2,1:T(8,128)(2,1)} %bitcast.28), calls=%async_computation.1 | async-start | bytes 1048576 | tf_op jit(solution)/shard_map/all_to_all | solution.py:82
  153.7 6.9 %pad_maximum_fusion = (bf16[128,2048]{0,1:T(8,128)(2,1)S(1)}, bf16[128,2048]{0,1:T(8,128)(2,1)S(1)}, bf16[128,2048]{0,1:T(8,128)(2,1)S(1)}, bf16[128,2048]{0,1:T...) fusion(bf16[128,2048]{0,1:T(8,128)(2,1)} %bitcast.13, ...), kind=kLoop, calls=%fused_computation.105 | loop fusion | flops 8388608 | bytes 4751360 | tf_op jit(solution)/shard_map/concatenate | solution.py:16
  161.0 0.8 copy-done.7
  162.2 0.9 copy-done.5
  163.4 0.9 copy-done.12
  165.0 0.9 copy-done.3
  166.2 0.9 copy-done.1
  167.8 0.8 copy-done.15
  168.6 1.3 convolution_add_fusion.1
  170.0 1.6 copy.191
  171.5 1.1 copy.166
  172.7 1.3 reshape.83
  174.0 1.4 fusion.10
  178.0 1.9 copy.171
  180.0 2.4 copy.284
  182.7 0.7 copy-done.17
  183.8 1.9 convolution_multiply_fusion
  185.7 39.9 %all-reduce.1 = f32[2048]{0:T(1024)S(1)} all-reduce(f32[2048]{0:T(1024)S(1)} %broadcast_multiply_fusion.1), channel_id=3, replica_groups=mesh['fsdp'=4,'seq'=8] {'fsdp','seq'}, use_global_device_ids=true, to_apply=%region_4.5.clone | all-reduce | flops 2048 | bytes 16384
  226.2 11.7 %all-reduce.4.cloned.1.call-done = f32[256,1152]{0,1:T(8,128)} async-done(((f32[256,1152]{0,1:T(8,128)}), f32[256,1152]{0,1:T(8,128)}) %all-reduce.4.cloned.1.call-update) | async-done | bytes 1179664 | tf_op jit(solution)/shard_map/psum | solution.py:115
  237.9 2.7 copy.172
  240.6 137.1 %reduce-scatter.2.cloned.1.call-done = f32[8,2048]{1,0:T(8,128)} async-done(((f32[256,2048]{1,0:T(8,128)}), f32[8,2048]{1,0:T(8,128)}) %reduce-scatter.2.cloned.1.call-update) | async-done | bytes 65552 | tf_op jit(solution)/shard_map/reduce_scatter | solution.py:130
  (97 shorter events, 13.1 us)
Async XLA Ops:
  7.2 32.1 %copy-start.30 = (s32[1,128]{1,0:T(1,128)S(1)}, s32[1,128]{1,0:T(1,128)}, u32[]{:S(2)}) copy-start(s32[1,128]{1,0:T(1,128)} %param.7) | copy-start | bytes 1540
  7.2 32.1 %copy-start.26 = (bf16[1,128,2048]{2,1,0:T(8,128)(2,1)S(1)}, bf16[1,128,2048]{2,1,0:T(8,128)(2,1)}, u32[]{:S(2)}) copy-start(bf16[1,128,2048]{2,1,0:T(8,128)(2,1)} %param.6) | copy-start | bytes 1572868
  7.2 32.0 %all-gather.3.cloned.1.call-start = ((), (), s32[]{:S(2)}) async-start(), calls=%async_computation.3 | async-start | bytes 1310720 | tf_op jit(solution)/shard_map/all_gather | solution.py:41
  7.9 90.2 %all-gather.5.cloned.1.call-start = ((), (), s32[]{:S(2)}) async-start(), calls=%async_computation.4 | async-start | bytes 5898240 | tf_op jit(solution)/shard_map/all_gather | solution.py:52
  39.2 1.7 copy-start.29
  41.1 9.4 %copy-start.16 = (bf16[1,128,2048]{2,1,0:T(8,128)(2,1)S(1)}, bf16[1,128,2048]{2,1,0:T(8,128)(2,1)}, u32[]{:S(2)}) copy-start(bf16[1,128,2048]{2,1,0:T(8,128)(2,1)} %param.11) | copy-start | bytes 1572868
  42.1 20.0 %all-to-all-start.1 = ((bf16[128,8,256]{0,2,1:T(8,128)(2,1)}), bf16[128,8,256]{0,2,1:T(8,128)(2,1)S(1)}, u32[]{:S(2)}, u32[]{:S(2)}) async-start(bf16[128,8,256]{0,2,1:T(8,128)(2,1)} %bitcast.30), calls=%async_computation.2 | async-start | bytes 1048576 | tf_op jit(solution)/shard_map/all_to_all | solution.py:81
  46.7 5.0 %collective-permute-start = (bf16[4,2048]{1,0:T(4,128)(2,1)S(1)}, bf16[4,2048]{1,0:T(4,128)(2,1)S(1)}, u32[]{:S(2)}, u32[]{:S(2)}) collective-permute-start(bf16[4,2048]{1,0:T(4,128)(2,1)S(1)} %get-tuple-element.54), channel_id=1, source_target_pairs={{0,1},{1,2},{2,3},{3,4},{4,5},{5,6},{6,7},{8,9},{9,10},{10,11},{11... | collective-permute-start | bytes 49160 | tf_op jit(solution)/shard_map/ppermute | solution.py:18
  49.1 4.2 %collective-permute-start.1 = (bf16[4,2048]{1,0:T(4,128)(2,1)S(1)}, bf16[4,2048]{1,0:T(4,128)(2,1)S(1)}, u32[]{:S(2)}, u32[]{:S(2)}) collective-permute-start(bf16[4,2048]{1,0:T(4,128)(2,1)S(1)} %get-tuple-element.53), channel_id=1, source_target_pairs={{1,0},{2,1},{3,2},{4,3},{5,4},{6,5},{7,6},{9,8},{10,9},{11,10},{12... | collective-permute-start | bytes 49160 | tf_op jit(solution)/shard_map/ppermute | solution.py:20
  108.6 19.9 %copy-start.23 = (bf16[16,16,8,128]{3,2,1,0:T(8,128)(2,1)S(1)}, bf16[16,16,8,128]{3,2,1,0:T(8,128)(2,1)}, u32[]{:S(2)}) copy-start(bf16[16,16,8,128]{3,2,1,0:T(8,128)(2,1)} %get-tuple-element.51) | copy-start | bytes 1572868
  128.4 2.0 copy-start.6
  128.4 2.0 copy-start.8
  128.5 2.0 copy-start.4
  128.5 3.4 copy-start.11
  128.5 4.6 %copy-start.10 = (bf16[16,128,1,128]{3,2,1,0:T(2,128)(2,1)}, bf16[16,128,1,128]{3,2,1,0:T(2,128)(2,1)S(1)}, u32[]{:S(2)}) copy-start(bf16[16,128,1,128]{3,2,1,0:T(2,128)(2,1)S(1)} %get-tuple-element.22) | copy-start | bytes 1572868
  128.5 5.1 %copy-start.2 = (bf16[16,128,1,128]{3,2,1,0:T(2,128)(2,1)}, bf16[16,128,1,128]{3,2,1,0:T(2,128)(2,1)S(1)}, u32[]{:S(2)}) copy-start(bf16[16,128,1,128]{3,2,1,0:T(2,128)(2,1)S(1)} %get-tuple-element.21) | copy-start | bytes 1572868
  128.5 6.1 %copy-start = (bf16[16,128,1,128]{3,2,1,0:T(2,128)(2,1)}, bf16[16,128,1,128]{3,2,1,0:T(2,128)(2,1)S(1)}, u32[]{:S(2)}) copy-start(bf16[16,128,1,128]{3,2,1,0:T(2,128)(2,1)S(1)} %get-tuple-element.20) | copy-start | bytes 1572868
  128.5 7.6 %copy-start.14 = (bf16[16,128,1,128]{3,2,1,0:T(2,128)(2,1)}, bf16[16,128,1,128]{3,2,1,0:T(2,128)(2,1)S(1)}, u32[]{:S(2)}) copy-start(bf16[16,128,1,128]{3,2,1,0:T(2,128)(2,1)S(1)} %get-tuple-element.18) | copy-start | bytes 1572868
  128.5 1.4 copy-start.22
  129.9 1.4 copy-start.21
  131.3 1.2 copy-start.20
  133.0 1.0 copy-start.19
  134.1 1.0 copy-start.18
  135.6 1.2 copy-start.25
  135.6 1.3 copy-start.27
  138.9 14.8 %collective-permute-start.2 = (bf16[4,2048]{0,1:T(8,128)(2,1)}, bf16[4,2048]{0,1:T(8,128)(2,1)}, u32[]{:S(2)}, u32[]{:S(2)}) collective-permute-start(bf16[4,2048]{0,1:T(8,128)(2,1)} %copy.145), channel_id=1, source_target_pairs={{1,0},{2,1},{3,2},{4,3},{5,4},{6,5},{7,6},{9,8},{10,9},{11,10},{12... | collective-permute-start | bytes 49160 | tf_op jit(solution)/shard_map/ppermute | solution.py:20
  141.3 12.4 %collective-permute-start.3 = (bf16[4,2048]{0,1:T(8,128)(2,1)}, bf16[4,2048]{0,1:T(8,128)(2,1)}, u32[]{:S(2)}, u32[]{:S(2)}) collective-permute-start(bf16[4,2048]{0,1:T(8,128)(2,1)} %copy.155), channel_id=1, source_target_pairs={{0,1},{1,2},{2,3},{3,4},{4,5},{5,6},{6,7},{8,9},{9,10},{10,11},{11... | collective-permute-start | bytes 49160 | tf_op jit(solution)/shard_map/ppermute | solution.py:18
  148.8 22.7 %all-to-all-start = ((bf16[128,8,256]{0,2,1:T(8,128)(2,1)}), bf16[128,8,256]{0,2,1:T(8,128)(2,1)S(1)}, u32[]{:S(2)}, u32[]{:S(2)}) async-start(bf16[128,8,256]{0,2,1:T(8,128)(2,1)} %bitcast.28), calls=%async_computation.1 | async-start | bytes 1048576 | tf_op jit(solution)/shard_map/all_to_all | solution.py:82
  153.5 84.4 %all-reduce.4.cloned.1.call-start = ((), (), s32[]{:S(2)}) async-start(), calls=%async_computation.6 | async-start | bytes 2359296 | tf_op jit(solution)/shard_map/psum | solution.py:115
  153.7 6.9 %copy-start.9 = (bf16[16,128,1,128]{3,2,1,0:T(2,128)(2,1)S(1)}, bf16[16,128,1,128]{3,2,1,0:T(2,128)(2,1)}, u32[]{:S(2)}) copy-start(bf16[16,128,1,128]{3,2,1,0:T(2,128)(2,1)} %copy-done.8) | copy-start | bytes 1572868
  160.6 1.2 copy-start.7
  161.8 1.2 copy-start.5
  163.1 1.2 copy-start.12
  163.1 1.5 copy-start.13
  164.6 1.2 copy-start.3
  165.8 1.2 copy-start.1
  167.4 1.2 copy-start.15
  173.9 1.4 copy-start.28
  182.3 1.0 copy-start.17
  182.4 195.3 %reduce-scatter.2.cloned.1.call-start = ((), (), s32[]{:S(2)}) async-start(), calls=%async_computation.5 | async-start | bytes 2162688 | tf_op jit(solution)/shard_map/reduce_scatter | solution.py:130
  183.8 1.9 copy-start.24
Sparse Core Ops, SparseCore 0:
  9.9 29.3 all-gather.2
  41.1 57.0 all-gather.4
  182.5 55.3 all-reduce.3
  240.7 136.9 reduce-scatter.1
where the time goes:
time: 386 us; the launch traced here: 384 us
  waiting for transfers between devices  223 us (58%)
  local copies, waits for them, and re-layouts  59.2 us (15%)
  blocking collectives  39.9 us (10%)
  matrix products  18.8 us (5%)
  starting transfers between devices  18.4 us (5%)
  between operations  14.4 us (4%)
  other arithmetic  10.6 us (3%)
    reduce_scatter x1, waiting for transfers between devices, body(): lax.psum_scatter(table_term, ('fsdp', 'seq'), scatter_dimension=0, tiled=...  137 us
    unnamed x1, blocking collectives  39.9 us
    all_gather x1, waiting for transfers between devices, body(): lax.all_gather(kernel, 'fsdp', axis=0, tiled=True)  34.5 us
    all_gather x1, waiting for transfers between devices, body(): table = lax.all_gather(type_table, 'fsdp', axis=0, tiled=True)  30.6 us
    slice x1, local copies, waits for them, and re-layouts, body(): weights[:, :, k, :]  19.8 us
    unnamed x66, local copies, waits for them, and re-layouts  17.4 us
    psum x1, waiting for transfers between devices, body(): kernel_grad = lax.psum(kernel_part, 'fsdp')  11.7 us
    reshape x1, local copies, waits for them, and re-layouts, body(): lax.all_gather(kernel, 'fsdp', axis=0, tiled=True)  10.5 us
  transfers between devices with their start and end apart: 10, of which 6 were waited for; matrix products, arithmetic and copies ran while one was open for 8% of the time, Pallas kernels for 0%

commit v1 on v0

--- a/solution.py
+++ b/solution.py
@@ -5,6 +5,10 @@
 
 GROUPS = 16
 KERNEL = 9
+
+
+def mix_groups_in(load, which_axis):
+    return jnp.sum(lax.all_gather(load, axis_name=which_axis), axis=0)
 
 
 def with_halo(cells, sides, width):
@@ -112,7 +116,7 @@
             )
         )
     kernel_part = jnp.stack(kterms, axis=2).reshape(slice_width, KERNEL * chans) * scale
-    kernel_grad = lax.psum(kernel_part, "fsdp")
+    kernel_grad = mix_groups_in(kernel_part, which_axis="fsdp")
     dnormed = dnormed.reshape(length, width)
     gain_term = jnp.sum(dnormed * mixed * inv, axis=0) * scale
     scaled = norm_gain * dnormed

time: 386 us -> 369 us (0.956)
  waiting for transfers between devices: 223 us -> 206 us
  local copies, waits for them, and re-layouts: 59.2 us -> 51.8 us
  blocking collectives: 39.9 us -> 46.3 us
    reduce_scatter x1, waiting for transfers between devices: 137 us -> 118 us  [body(): lax.psum_scatter(table_term, ('fsdp', 'seq'), scatter_dimension=0, tiled=...]
    all_to_all x1, waiting for transfers between devices: 0.01 us -> 13.5 us  [body(): lax.all_to_all(dflat, 'seq', split_axis=1, concat_axis=0, tiled=True)]
    psum x1 -> x0, waiting for transfers between devices: 11.7 us -> none  [body(): kernel_grad = lax.psum(kernel_part, 'fsdp')]
    all_gather x1, waiting for transfers between devices: 34.5 us -> 42 us  [body(): lax.all_gather(kernel, 'fsdp', axis=0, tiled=True)]
    unnamed x1, blocking collectives: 39.9 us -> 46.3 us
    all_to_all x1, waiting for transfers between devices: 6.03 us -> 0.01 us  [body(): lax.all_to_all(normed, 'seq', split_axis=1, concat_axis=0, tiled=True)]
    unnamed x66 -> x70, local copies, waits for them, and re-layouts: 17.4 us -> 12.6 us
  transfers between devices with their start and end apart: 10 -> 10, of which waited for: 6 -> 5; matrix products, arithmetic and copies ran while one was open for 8% -> 17% of each run, Pallas kernels for 0% -> 0%
where the time goes in v1:
time: 369 us; the launch traced here: 367 us
  waiting for transfers between devices  206 us (56%)
  local copies, waits for them, and re-layouts  51.8 us (14%)
  blocking collectives  46.3 us (13%)
  starting transfers between devices  19.5 us (5%)
  matrix products  15.5 us (4%)
  between operations  14.4 us (4%)
  other arithmetic  13.3 us (4%)
    reduce_scatter x1, waiting for transfers between devices, body(): lax.psum_scatter(table_term, ('fsdp', 'seq'), scatter_dimension=0, tiled=...  118 us
    unnamed x1, blocking collectives  46.3 us
    all_gather x1, waiting for transfers between devices, body(): lax.all_gather(kernel, 'fsdp', axis=0, tiled=True)  42 us
    all_gather x1, waiting for transfers between devices, body(): table = lax.all_gather(type_table, 'fsdp', axis=0, tiled=True)  30.6 us
    slice x1, local copies, waits for them, and re-layouts, body(): weights[:, :, k, :]  19.9 us
    all_to_all x1, waiting for transfers between devices, body(): lax.all_to_all(dflat, 'seq', split_axis=1, concat_axis=0, tiled=True)  13.5 us
    unnamed x70, local copies, waits for them, and re-layouts  12.6 us
    reshape x1, local copies, waits for them, and re-layouts, body(): lax.all_gather(kernel, 'fsdp', axis=0, tiled=True)  10.5 us
  transfers between devices with their start and end apart: 10, of which 5 were waited for; matrix products, arithmetic and copies ran while one was open for 17% of the time, Pallas kernels for 0%

profile of v1, /device:TPU:0, one launch (start us, length us, event | category | flops | bytes accessed | tf_op | source)
XLA Modules:
  0.0 367.2 jit_solution(5028256366065421682)
XLA Ops:
  7.2 0.7 all-gather.4.cloned.1.call-update
  8.0 0.7 all-gather.6.cloned.1.call-update
  8.7 30.6 %all-gather.4.cloned.1.call-done = bf16[256,2048]{1,0:T(8,128)(2,1)} async-done(((bf16[64,2048]{1,0:T(8,128)(2,1)}), bf16[256,2048]{1,0:T(8,128)(2,1)}) %all-gather.4.cloned.1.call-update) | async-done | bytes 1048592 | tf_op jit(solution)/shard_map/all_gather | solution.py:45
  39.2 1.7 multiply_reduce_fusion.2
  41.1 1.7 collective-permute-start
  42.9 1.3 collective-permute-start.1
  44.3 1.2 copy.216
  45.4 1.0 copy.192
  46.4 7.1 %all-to-all-start.1 = ((bf16[128,8,256]{0,2,1:T(8,128)(2,1)}), bf16[128,8,256]{0,2,1:T(8,128)(2,1)S(1)}, u32[]{:S(2)}, u32[]{:S(2)}) async-start(bf16[128,8,256]{0,2,1:T(8,128)(2,1)} %bitcast.30), calls=%async_computation.2 | async-start | bytes 1048576 | tf_op jit(solution)/shard_map/all_to_all | solution.py:85
  53.6 2.6 fusion.52
  56.2 42.0 %all-gather.6.cloned.1.call-done = bf16[2048,1152]{1,0:T(8,128)(2,1)} async-done(((bf16[512,1152]{1,0:T(8,128)(2,1)}), bf16[2048,1152]{1,0:T(8,128)(2,1)}) %all-gather.6.cloned.1.call-update) | async-done | bytes 4718608 | tf_op jit(solution)/shard_map/all_gather | solution.py:56
  98.2 10.5 %reshape.99 = bf16[16,128,9,128]{3,2,1,0:T(8,128)(2,1)} reshape(bf16[2048,1152]{1,0:T(8,128)(2,1)} %all-gather.6.cloned.1.call-done) | data formatting | bytes 9437184 | tf_op jit(solution)/shard_map/reshape | solution.py:56
  108.6 19.9 %fusion.82 = (bf16[16,128,1,128]{3,2,1,0:T(2,128)(2,1)S(1)}, bf16[16,128,1,128]{3,2,1,0:T(2,128)(2,1)S(1)}, bf16[16,128,1,128]{3,2,1,0:T(2,128)(2,1)S(1)}, bf16[...) fusion(bf16[16,128,9,128]{3,2,1,0:T(8,128)(2,1)} %reshape.99), kind=kLoop, calls=%fused_computation.153 | loop fusion | bytes 9437184 | tf_op jit(solution)/shard_map/slice | solution.py:64
  129.1 0.9 copy-done.25
  130.6 0.9 copy-done.24
  132.0 0.9 copy-done.23
  133.4 0.5 convolution_add_fusion.12
  134.9 0.5 convolution_add_fusion.10
  135.5 0.5 convolution_add_fusion.9
  136.0 0.7 copy-done.28
  136.8 0.8 fusion.14
  137.7 1.0 copy.142
  138.7 4.6 %all-to-all-start = ((bf16[128,8,256]{0,2,1:T(8,128)(2,1)}), bf16[128,8,256]{0,2,1:T(8,128)(2,1)S(1)}, u32[]{:S(2)}, u32[]{:S(2)}) async-start(bf16[128,8,256]{0,2,1:T(8,128)(2,1)} %bitcast.28), calls=%async_computation.1 | async-start | bytes 1048576 | tf_op jit(solution)/shard_map/all_to_all | solution.py:86
  144.1 1.0 copy.167
  145.1 13.5 %all-to-all-done = bf16[128,8,256]{0,2,1:T(8,128)(2,1)S(1)} async-done(((bf16[128,8,256]{0,2,1:T(8,128)(2,1)}), bf16[128,8,256]{0,2,1:T(8,128)(2,1)S(1)}, u32[]{:S(2)}, u32[]{:S(2)}) %all-to-all-start) | async-done | bytes 524320 | tf_op jit(solution)/shard_map/all_to_all | solution.py:86
  159.2 1.4 fusion.10
  163.2 0.7 copy.193
  164.0 1.2 reshape.98
  165.3 0.9 slice_bitcast_fusion
  166.5 1.3 collective-permute-start.2
  167.8 1.1 copy.153
  168.9 3.1 collective-permute-start.3
  172.0 0.5 fusion.63
  172.5 1.2 collective-permute-done.3
  173.7 5.9 %pad_maximum_fusion = (bf16[128,2048]{0,1:T(8,128)(2,1)S(1)}, bf16[128,2048]{0,1:T(8,128)(2,1)S(1)}, bf16[128,2048]{0,1:T(8,128)(2,1)S(1)}, bf16[128,2048]{0,1:T...) fusion(bf16[128,2048]{0,1:T(8,128)(2,1)} %bitcast.13, ...), kind=kLoop, calls=%fused_computation.104 | loop fusion | flops 8388608 | bytes 4751360 | tf_op jit(solution)/shard_map/concatenate | solution.py:20
  180.0 0.8 copy-done.9
  181.2 0.9 copy-done.7
  182.4 0.9 copy-done.15
  183.6 0.9 copy-done.5
  184.9 0.9 copy-done.3
  186.1 0.9 copy-done.1
  187.3 0.9 copy-done.17
  189.2 0.7 copy-done.21
  190.3 1.9 convolution_multiply_fusion
  192.3 46.3 %all-reduce.1 = f32[2048]{0:T(1024)S(1)} all-reduce(f32[2048]{0:T(1024)S(1)} %broadcast_multiply_fusion.1), channel_id=3, replica_groups=mesh['fsdp'=4,'seq'=8] {'fsdp','seq'}, use_global_device_ids=true, to_apply=%region_4.5.clone | all-reduce | flops 2048 | bytes 16384
  238.6 0.6 dynamic-slice
  239.2 3.7 %reduce_sum.39 = f32[256,1152]{1,0:T(8,128)} reduce(f32[4,256,1152]{2,1,0:T(8,128)} %all-gather.8.cloned.1.call-done, f32[]{:T(128)} %constant.6.clone.1), dimensions={0}, to_apply=%region_5.6 | reduce | flops 884736 | bytes 5898244 | tf_op jit(solution)/shard_map/reduce_sum | solution.py:11
  242.9 117.8 %reduce-scatter.2.cloned.1.call-done = f32[8,2048]{1,0:T(8,128)} async-done(((f32[256,2048]{1,0:T(8,128)}), f32[8,2048]{1,0:T(8,128)}) %reduce-scatter.2.cloned.1.call-update) | async-done | bytes 65552 | tf_op jit(solution)/shard_map/reduce_scatter | solution.py:134
  (103 shorter events, 11.7 us)
Async XLA Ops:
  7.2 32.1 %copy-start.33 = (s32[1,128]{1,0:T(1,128)S(1)}, s32[1,128]{1,0:T(1,128)}, u32[]{:S(2)}) copy-start(s32[1,128]{1,0:T(1,128)} %param.7) | copy-start | bytes 1540
  7.2 32.1 %copy-start.29 = (bf16[1,128,2048]{2,1,0:T(8,128)(2,1)S(1)}, bf16[1,128,2048]{2,1,0:T(8,128)(2,1)}, u32[]{:S(2)}) copy-start(bf16[1,128,2048]{2,1,0:T(8,128)(2,1)} %param.6) | copy-start | bytes 1572868
  7.2 32.0 %all-gather.4.cloned.1.call-start = ((), (), s32[]{:S(2)}) async-start(), calls=%async_computation.3 | async-start | bytes 1310720 | tf_op jit(solution)/shard_map/all_gather | solution.py:45
  7.9 90.2 %all-gather.6.cloned.1.call-start = ((), (), s32[]{:S(2)}) async-start(), calls=%async_computation.4 | async-start | bytes 5898240 | tf_op jit(solution)/shard_map/all_gather | solution.py:56
  39.2 1.7 copy-start.32
  40.9 3.3 copy-start.20
  41.1 12.5 %collective-permute-start = (bf16[4,2048]{1,0:T(4,128)(2,1)S(1)}, bf16[4,2048]{1,0:T(4,128)(2,1)S(1)}, u32[]{:S(2)}, u32[]{:S(2)}) collective-permute-start(bf16[4,2048]{1,0:T(4,128)(2,1)S(1)} %get-tuple-element.46), channel_id=1, source_target_pairs={{0,1},{1,2},{2,3},{3,4},{4,5},{5,6},{6,7},{8,9},{9,10},{10,11},{11... | collective-permute-start | bytes 49160 | tf_op jit(solution)/shard_map/ppermute | solution.py:22
  42.9 10.7 %collective-permute-start.1 = (bf16[4,2048]{1,0:T(4,128)(2,1)S(1)}, bf16[4,2048]{1,0:T(4,128)(2,1)S(1)}, u32[]{:S(2)}, u32[]{:S(2)}) collective-permute-start(bf16[4,2048]{1,0:T(4,128)(2,1)S(1)} %get-tuple-element.45), channel_id=1, source_target_pairs={{1,0},{2,1},{3,2},{4,3},{5,4},{6,5},{7,6},{9,8},{10,9},{11,10},{12... | collective-permute-start | bytes 49160 | tf_op jit(solution)/shard_map/ppermute | solution.py:24
  46.4 92.3 %all-to-all-start.1 = ((bf16[128,8,256]{0,2,1:T(8,128)(2,1)}), bf16[128,8,256]{0,2,1:T(8,128)(2,1)S(1)}, u32[]{:S(2)}, u32[]{:S(2)}) async-start(bf16[128,8,256]{0,2,1:T(8,128)(2,1)} %bitcast.30), calls=%async_computation.2 | async-start | bytes 1048576 | tf_op jit(solution)/shard_map/all_to_all | solution.py:85
  108.6 20.0 %copy-start.26 = (bf16[16,16,8,128]{3,2,1,0:T(8,128)(2,1)S(1)}, bf16[16,16,8,128]{3,2,1,0:T(8,128)(2,1)}, u32[]{:S(2)}) copy-start(bf16[16,16,8,128]{3,2,1,0:T(8,128)(2,1)} %get-tuple-element.43) | copy-start | bytes 1572868
  128.5 2.0 copy-start.8
  128.5 2.0 copy-start.6
  128.6 3.4 copy-start.10
  128.6 3.4 copy-start.14
  128.6 4.8 %copy-start.12 = (bf16[16,128,1,128]{3,2,1,0:T(2,128)(2,1)}, bf16[16,128,1,128]{3,2,1,0:T(2,128)(2,1)S(1)}, u32[]{:S(2)}) copy-start(bf16[16,128,1,128]{3,2,1,0:T(2,128)(2,1)S(1)} %get-tuple-element.14) | copy-start | bytes 1572868
  128.6 5.4 %copy-start.4 = (bf16[16,128,1,128]{3,2,1,0:T(2,128)(2,1)}, bf16[16,128,1,128]{3,2,1,0:T(2,128)(2,1)S(1)}, u32[]{:S(2)}) copy-start(bf16[16,128,1,128]{3,2,1,0:T(2,128)(2,1)S(1)} %get-tuple-element.13) | copy-start | bytes 1572868
  128.6 6.3 %copy-start.2 = (bf16[16,128,1,128]{3,2,1,0:T(2,128)(2,1)}, bf16[16,128,1,128]{3,2,1,0:T(2,128)(2,1)S(1)}, u32[]{:S(2)}) copy-start(bf16[16,128,1,128]{3,2,1,0:T(2,128)(2,1)S(1)} %get-tuple-element.12) | copy-start | bytes 1572868
  128.6 6.8 %copy-start = (bf16[16,128,1,128]{3,2,1,0:T(2,128)(2,1)}, bf16[16,128,1,128]{3,2,1,0:T(2,128)(2,1)S(1)}, u32[]{:S(2)}) copy-start(bf16[16,128,1,128]{3,2,1,0:T(2,128)(2,1)S(1)} %get-tuple-element.11) | copy-start | bytes 1572868
  128.6 7.4 %copy-start.16 = (bf16[16,128,1,128]{3,2,1,0:T(2,128)(2,1)}, bf16[16,128,1,128]{3,2,1,0:T(2,128)(2,1)S(1)}, u32[]{:S(2)}) copy-start(bf16[16,128,1,128]{3,2,1,0:T(2,128)(2,1)S(1)} %get-tuple-element.10) | copy-start | bytes 1572868
  128.6 1.4 copy-start.25
  130.1 1.4 copy-start.24
  131.5 1.4 copy-start.23
  133.4 1.0 copy-start.22
  135.4 1.2 copy-start.28
  135.5 1.3 copy-start.30
  137.7 5.9 %copy-start.18 = (bf16[128,16,128]{2,0,1:T(8,128)(2,1)}, bf16[128,16,128]{2,0,1:T(8,128)(2,1)S(1)}, u32[]{:S(2)}) copy-start(bf16[128,16,128]{2,0,1:T(8,128)(2,1)S(1)} %fusion.14) | copy-start | bytes 1572868
  138.7 20.0 %all-to-all-start = ((bf16[128,8,256]{0,2,1:T(8,128)(2,1)}), bf16[128,8,256]{0,2,1:T(8,128)(2,1)S(1)}, u32[]{:S(2)}, u32[]{:S(2)}) async-start(bf16[128,8,256]{0,2,1:T(8,128)(2,1)} %bitcast.28), calls=%async_computation.1 | async-start | bytes 1048576 | tf_op jit(solution)/shard_map/all_to_all | solution.py:86
  143.3 95.9 %all-gather.8.cloned.1.call-start = ((), (), s32[]{:S(2)}) async-start(), calls=%async_computation.6 | async-start | bytes 5898240 | tf_op jit(solution)/shard_map/all_gather | solution.py:11
  159.0 1.6 copy-start.31
  165.2 6.7 %copy-start.13 = (bf16[16,128,1,128]{3,2,1,0:T(2,128)(2,1)S(1)}, bf16[16,128,1,128]{3,2,1,0:T(2,128)(2,1)}, u32[]{:S(2)}) copy-start(bf16[16,128,1,128]{3,2,1,0:T(2,128)(2,1)} %copy-done.12) | copy-start | bytes 1572868
  165.2 6.8 %copy-start.19 = (bf16[128,16,128]{2,0,1:T(8,128)(2,1)S(1)}, bf16[128,16,128]{2,0,1:T(8,128)(2,1)}, u32[]{:S(2)}) copy-start(bf16[128,16,128]{2,0,1:T(8,128)(2,1)} %copy-done.18) | copy-start | bytes 1572868
  165.2 195.5 %reduce-scatter.2.cloned.1.call-start = ((), (), s32[]{:S(2)}) async-start(), calls=%async_computation.5 | async-start | bytes 2162688 | tf_op jit(solution)/shard_map/reduce_scatter | solution.py:134
  166.5 6.0 %collective-permute-start.2 = (bf16[4,2048]{0,1:T(8,128)(2,1)S(1)}, bf16[4,2048]{0,1:T(8,128)(2,1)}, u32[]{:S(2)}, u32[]{:S(2)}) collective-permute-start(bf16[4,2048]{0,1:T(8,128)(2,1)S(1)} %copy.143), channel_id=1, source_target_pairs={{1,0},{2,1},{3,2},{4,3},{5,4},{6,5},{7,6},{9,8},{10,9},{11,10},{12... | collective-permute-start | bytes 49160 | tf_op jit(solution)/shard_map/ppermute | solution.py:24
  168.9 4.8 %collective-permute-start.3 = (bf16[4,2048]{0,1:T(8,128)(2,1)}, bf16[4,2048]{0,1:T(8,128)(2,1)S(1)}, u32[]{:S(2)}, u32[]{:S(2)}) collective-permute-start(bf16[4,2048]{0,1:T(8,128)(2,1)} %copy.153), channel_id=1, source_target_pairs={{0,1},{1,2},{2,3},{3,4},{4,5},{5,6},{6,7},{8,9},{9,10},{10,11},{11... | collective-permute-start | bytes 49160 | tf_op jit(solution)/shard_map/ppermute | solution.py:22
  173.7 5.9 %copy-start.11 = (bf16[16,128,1,128]{3,2,1,0:T(2,128)(2,1)S(1)}, bf16[16,128,1,128]{3,2,1,0:T(2,128)(2,1)}, u32[]{:S(2)}) copy-start(bf16[16,128,1,128]{3,2,1,0:T(2,128)(2,1)} %copy-done.10) | copy-start | bytes 1572868
  179.6 1.2 copy-start.9
  180.8 1.2 copy-start.7
  182.0 1.2 copy-start.15
  183.3 1.2 copy-start.5
  184.5 1.2 copy-start.3
  185.7 1.2 copy-start.1
  186.9 1.2 copy-start.17
  188.9 1.0 copy-start.21
  190.3 1.9 copy-start.27
Sparse Core Ops, SparseCore 0:
  9.9 29.3 all-gather.3
  41.1 57.0 all-gather.5
  165.4 55.6 all-gather.7
  223.8 136.8 reduce-scatter.1
